TPU v7x, 256 devices: a whole 4x4x8 slice. The times are simulated.
256 devices in a mesh: space: 16 (over z_lo, y), view: 16 (over x, z_hi, core).
Axes of the slice: x: 4, y: 4, z: 8 (z_hi: 2, z_lo: 4; z = z_hi * 4 + z_lo), core: 2. Of those that a mesh axis runs over, the one named last changes fastest.
Arguments:
- estimate: float32 [16, 64, 4096], P('space', None, 'view'), may hold values from 0.5 to 2
- measured: float32 [16, 16, 64, 4096], P('view', 'space'), may hold values from 0.2 to 5
- kernel_x: float32 [16, 7], P('view'), may hold values from 0.2 to 1
- kernel_y: float32 [16, 7], P('view'), may hold values from 0.2 to 1
- kernel_z: float32 [16, 15], P('view'), may hold values from 0.2 to 1
- neighbors: int32 [16, 6], P('space'), may hold values from -1 to 15, as said below
- inside: int32 [16], P('space'), may hold values 0 or 1
Outputs:
- deconvolved: float32 [16, 64, 4096], P('space', None, 'view')
Inputs may be any that keep to these rules, and one draw needn't show every extreme that they name: neighbors[b, f] is the brick across face f of brick b (faces in order: low and high along the first, second and third cell dimension), or -1 at the window's border; if neighbors[b, f] = c then neighbors[c, f + 1 - 2 (f % 2)] = b; the window is a box of 2 x 2 x (4) bricks, and the 1 bricks of one index of space lie in a row along the third dimension.
All inputs are finite; a program needn't handle non-finite values. No bound on the sum of `inside` on one device may be relied on, other than what follows from the above.
Results may differ from a plain program's by a relative error of at most 0.0001.
Values sent between devices are 32-bit elements; how exact they have to be, the bound alone decides.
No kernel may reach another device: no remote copies, remote signals or barrier semaphores. Data moves between devices by JAX's collectives and lax.ppermute only.
A program may use at most 128 MiB of HBM per device.

v0:
```python
import jax
import jax.numpy as jnp
from jax import lax
from jax.sharding import PartitionSpec as P

ITERS = 2


def normalized(kernel):
    return kernel / jnp.sum(kernel)


def edge_planes(volume, axis_dim, radius):
    length = volume.shape[axis_dim]
    first_part = lax.slice_in_dim(volume, 0, radius, axis=axis_dim)
    last_part = lax.slice_in_dim(volume, length - radius, length, axis=axis_dim)
    stacked = jnp.stack([first_part, last_part], axis=1)
    return jnp.moveaxis(stacked, axis_dim + 1, 2)


def pick_faces(neighbors, axis_dim):
    low_ids = neighbors[:, 2 * axis_dim - 2]
    high_ids = neighbors[:, 2 * axis_dim - 1]

    def fold_faces(running, incoming, first_row):
        count_rows = incoming.shape[0]
        brick_ids = jnp.arange(count_rows, dtype=jnp.int32)
        low_pick = (low_ids[:, None] == brick_ids[None, :]).astype(jnp.float32)
        high_pick = (high_ids[:, None] == brick_ids[None, :]).astype(jnp.float32)
        low_part = jnp.einsum(
            "br,rpac->bpac", low_pick, incoming[:, 1], precision=lax.Precision.HIGHEST
        )
        high_part = jnp.einsum(
            "br,rpac->bpac", high_pick, incoming[:, 0], precision=lax.Precision.HIGHEST
        )
        return jnp.stack([low_part, high_part], axis=1)

    return fold_faces


def with_halo(volume, neighbors, axis_dim, radius, source):
    edge_slabs = edge_planes(volume, axis_dim, radius)
    zeros_halo = jnp.zeros_like(edge_slabs)
    fold_faces = pick_faces(neighbors, axis_dim)
    if source == "estimate":
        halo_faces = fold_faces(
            zeros_halo, lax.all_gather(edge_slabs, "space", axis=0, tiled=True), jnp.int32(0)
        )
    elif source == "blurred":
        halo_faces = fold_faces(
            zeros_halo, lax.all_gather(edge_slabs, "space", axis=0, tiled=True), jnp.int32(0)
        )
    elif source == "blurred_z":
        halo_faces = fold_faces(
            zeros_halo, lax.all_gather(edge_slabs, "space", axis=0, tiled=True), jnp.int32(0)
        )
    elif source == "ratio_z":
        halo_faces = fold_faces(
            zeros_halo, lax.all_gather(edge_slabs, "space", axis=0, tiled=True), jnp.int32(0)
        )
    else:
        halo_faces = fold_faces(
            zeros_halo, lax.all_gather(edge_slabs, "space", axis=0, tiled=True), jnp.int32(0)
        )
    halo_faces = jnp.moveaxis(halo_faces, 2, axis_dim + 1)
    return jnp.concatenate([halo_faces[:, 0], volume, halo_faces[:, 1]], axis=axis_dim)


def convolve(extended, kernel, axis_dim, flipped):
    radius = (kernel.shape[0] - 1) // 2
    length = extended.shape[axis_dim] - 2 * radius
    out_shape = list(extended.shape)
    out_shape[axis_dim] = length
    summed = jnp.zeros(tuple(out_shape), jnp.float32)
    for position in range(2 * radius + 1):
        weight = kernel[2 * radius - position] if flipped else kernel[position]
        summed = summed + weight * lax.slice_in_dim(
            extended, position, position + length, axis=axis_dim
        )
    return summed


def shards(estimate, measured, kernel_x, kernel_y, kernel_z, neighbors, inside):
    brick_side = estimate.shape[1]
    share_cells = estimate.reshape(
        estimate.shape[0], brick_side, estimate.shape[2] // brick_side, brick_side
    )
    recorded_all = measured.reshape(
        measured.shape[0], measured.shape[1], brick_side, brick_side, brick_side
    )
    share_rows = share_cells.shape[2]
    row_start = lax.axis_index("view") * share_rows
    view_count = recorded_all.shape[0] * lax.axis_size("view")
    radius_x = (kernel_x.shape[1] - 1) // 2
    radius_y = (kernel_y.shape[1] - 1) // 2
    radius_z = (kernel_z.shape[1] - 1) // 2
    keep_mask = (inside > 0)[:, None, None, None]
    share_now = share_cells
    full_now = None
    for sweep_no in range(ITERS):
        if full_now is None:
            full_now = lax.all_gather(share_now, "view", axis=2, tiled=True)
            extended = with_halo(full_now, neighbors, 1, radius_x, "estimate")
        else:
            extended = with_halo(full_now, neighbors, 1, radius_x, "estimate")
        along_x = normalized(kernel_x[0])
        along_y = normalized(kernel_y[0])
        along_z = normalized(kernel_z[0])
        blurred = convolve(extended, along_x, 1, False)
        blurred = convolve(with_halo(blurred, neighbors, 2, radius_y, "blurred"), along_y, 2, False)
        blurred = convolve(
            with_halo(blurred, neighbors, 3, radius_z, "blurred_z"), along_z, 3, False
        )
        quotient = recorded_all[0] / blurred
        spread = convolve(with_halo(quotient, neighbors, 3, radius_z, "ratio_z"), along_z, 3, True)
        spread = convolve(with_halo(spread, neighbors, 2, radius_y, "ratio"), along_y, 2, True)
        spread = convolve(with_halo(spread, neighbors, 1, radius_x, "ratio"), along_x, 1, True)
        final_sweep = sweep_no == ITERS - 1
        if not final_sweep:
            summed = lax.psum(spread, "view")
            full_now = full_now * jnp.where(keep_mask, summed / view_count, 1.0)
        else:
            summed = lax.psum_scatter(spread, "view", scatter_dimension=2, tiled=True)
            own_rows = lax.dynamic_slice_in_dim(full_now, row_start, share_rows, 2)
            share_now = own_rows * jnp.where(keep_mask, summed / view_count, 1.0)
            full_now = None
    return share_now.reshape(share_now.shape[0], brick_side, share_rows * brick_side)


def solution(mesh):
    placed = (
        P("space", None, "view"),
        P("view", "space", None, None),
        P("view", None),
        P("view", None),
        P("view", None),
        P("space", None),
        P("space"),
    )
    return jax.shard_map(
        shards, mesh=mesh, in_specs=placed, out_specs=P("space", None, "view"), check_vma=False
    )
```

profile of v0, /device:TPU:8, one launch (start us, length us, event | category | flops | bytes accessed | tf_op | source)
XLA Modules:
  0.0 1770.8 jit_solution(11116695997213249861)
XLA Ops:
  8.3 67.6 %all-gather.14.cloned.1.call-done = f32[1,64,64,64]{3,1,0,2:T(8,128)} async-done(((f32[1,64,4,64]{3,1,0,2:T(8,128)}), f32[1,64,64,64]{3,1,0,2:T(8,128)}) %all-gather.14.cloned.1.call-update) | async-done | bytes 1048592 | tf_op jit(solution)/shard_map/all_gather | solution.py:102
  84.2 75.9 %all-gather.16.cloned.1.call-done = f32[16,2,3,64,64]{4,3,2,1,0:T(8,128)} async-done(((f32[1,2,3,64,64]{4,3,2,1,0:T(8,128)}), f32[16,2,3,64,64]{4,3,2,1,0:T(8,128)}) %all-gather.16.cloned.1.call-update) | async-done | bytes 1572880 | tf_op jit(solution)/shard_map/all_gather | solution.py:47
  177.2 82.1 %all-gather.18.cloned.1.call-done = f32[16,2,3,64,64]{4,3,2,1,0:T(8,128)} async-done(((f32[1,2,3,64,64]{4,3,2,1,0:T(8,128)}), f32[16,2,3,64,64]{4,3,2,1,0:T(8,128)}) %all-gather.18.cloned.1.call-update) | async-done | bytes 1572880 | tf_op jit(solution)/shard_map/all_gather | solution.py:51
  266.0 6.6 fusion.117
  287.2 88.8 %all-gather.20.cloned.1.call-done = f32[16,2,7,64,64]{4,3,2,1,0:T(8,128)} async-done(((f32[1,2,7,64,64]{4,3,2,1,0:T(8,128)}), f32[16,2,7,64,64]{4,3,2,1,0:T(8,128)}) %all-gather.20.cloned.1.call-update) | async-done | bytes 3670032 | tf_op jit(solution)/shard_map/all_gather | solution.py:55
  395.0 24.2 %fusion.239 = f32[1,64,64,64]{3,2,1,0:T(8,128)S(1)} fusion(f32[1,64,64,64]{3,2,1,0:T(8,128)S(1)} %copy-done.4, f32[1,64,64,7]{3,2,1,0:T(8,128)S(1)} %get-tuple-element.20, f32[1,64,64,64]{3,2,1,0:T(8,128)S(1)} %fusion.117, f32[1,64,64,7]{3,2,1,0:T(8,128)S(1)} %get-tuple-element.19, f32[]{:T(128)} %bitcast.96, f32[]{:T(128)} %bitcast.95, f32[]{:T(128)} %bitcast.94, ...), kind=kLoop, calls=%fused_computation.402 | loop fusion | flops 11534336 | bytes 3375164 | tf_op jit(solution)/shard_map/div | solution.py:114
  425.6 93.2 %all-gather.22.cloned.1.call-done = f32[16,2,7,64,64]{4,3,2,1,0:T(8,128)} async-done(((f32[1,2,7,64,64]{4,3,2,1,0:T(8,128)}), f32[16,2,7,64,64]{4,3,2,1,0:T(8,128)}) %all-gather.22.cloned.1.call-update) | async-done | bytes 3670032 | tf_op jit(solution)/shard_map/all_gather | solution.py:59
  539.5 36.4 %fusion.206 = f32[1,64,64,64]{3,2,1,0:T(8,128)} fusion(f32[1,64,64,7]{3,2,1,0:T(8,128)} %get-tuple-element.18, f32[1,64,64,64]{3,2,1,0:T(8,128)S(1)} %copy-done.3, f32[1,64,64,7]{3,2,1,0:T(8,128)} %get-tuple-element.17, f32[]{:T(128)} %bitcast.96, f32[]{:T(128)} %bitcast.95, f32[]{:T(128)} %bitcast.94, f32[]{:T(128)} %bitcast.93, f32[]{:T(128)} %bitcast.92, ...), kind=kLoop, calls=%fused_computation.343 | loop fusion | flops 11272192 | bytes 2326588 | tf_op jit(solution)/shard_map/add | solution.py:77
  577.8 84.3 %all-gather.24.cloned.1.call-done = f32[16,2,3,64,64]{4,3,2,1,0:T(8,128)} async-done(((f32[1,2,3,64,64]{4,3,2,1,0:T(8,128)}), f32[16,2,3,64,64]{4,3,2,1,0:T(8,128)}) %all-gather.24.cloned.1.call-update) | async-done | bytes 1572880 | tf_op jit(solution)/shard_map/all_gather | solution.py:63
  668.8 7.1 fusion.103
  676.7 84.3 %all-gather.26.cloned.1.call-done = f32[16,2,3,64,64]{4,3,2,1,0:T(8,128)} async-done(((f32[1,2,3,64,64]{4,3,2,1,0:T(8,128)}), f32[16,2,3,64,64]{4,3,2,1,0:T(8,128)}) %all-gather.26.cloned.1.call-update) | async-done | bytes 1572880 | tf_op jit(solution)/shard_map/all_gather | solution.py:63
  767.3 7.5 fusion.47
  775.6 199.1 %all-reduce.2.cloned.1.call-done = f32[1,64,64,64]{3,2,1,0:T(8,128)} async-done(((f32[1,64,64,64]{3,2,1,0:T(8,128)}), f32[1,64,64,64]{3,2,1,0:T(8,128)}) %all-reduce.2.cloned.1.call-update) | async-done | bytes 1048592 | tf_op jit(solution)/shard_map/psum | solution.py:120
  979.2 82.8 %all-gather.28.cloned.1.call-done = f32[16,2,3,64,64]{4,3,2,1,0:T(8,128)} async-done(((f32[1,2,3,64,64]{4,3,2,1,0:T(8,128)}), f32[16,2,3,64,64]{4,3,2,1,0:T(8,128)}) %all-gather.28.cloned.1.call-update) | async-done | bytes 1572880 | tf_op jit(solution)/shard_map/all_gather | solution.py:47
  1077.0 84.1 %all-gather.30.cloned.1.call-done = f32[16,2,3,64,64]{4,3,2,1,0:T(8,128)} async-done(((f32[1,2,3,64,64]{4,3,2,1,0:T(8,128)}), f32[16,2,3,64,64]{4,3,2,1,0:T(8,128)}) %all-gather.30.cloned.1.call-update) | async-done | bytes 1572880 | tf_op jit(solution)/shard_map/all_gather | solution.py:51
  1167.9 6.6 fusion.89
  1181.0 93.1 %all-gather.32.cloned.1.call-done = f32[16,2,7,64,64]{4,3,2,1,0:T(8,128)} async-done(((f32[1,2,7,64,64]{4,3,2,1,0:T(8,128)}), f32[16,2,7,64,64]{4,3,2,1,0:T(8,128)}) %all-gather.32.cloned.1.call-update) | async-done | bytes 3670032 | tf_op jit(solution)/shard_map/all_gather | solution.py:55
  1293.3 24.2 %fusion.166 = f32[1,64,64,64]{3,2,1,0:T(8,128)S(1)} fusion(f32[1,64,64,64]{3,2,1,0:T(8,128)S(1)} %copy-done.5, f32[1,64,64,7]{3,2,1,0:T(8,128)S(1)} %get-tuple-element.16, f32[1,64,64,64]{3,2,1,0:T(8,128)S(1)} %copy-done.1, f32[1,64,64,7]{3,2,1,0:T(8,128)S(1)} %get-tuple-element.15, f32[]{:T(128)} %bitcast.96, f32[]{:T(128)} %bitcast.95, f32[]{:T(128)} %bitcast.94, ...), kind=kLoop, calls=%fused_computation.269 | loop fusion | flops 11534336 | bytes 3375164 | tf_op jit(solution)/shard_map/div | solution.py:114
  1326.3 92.9 %all-gather.34.cloned.1.call-done = f32[16,2,7,64,64]{4,3,2,1,0:T(8,128)} async-done(((f32[1,2,7,64,64]{4,3,2,1,0:T(8,128)}), f32[16,2,7,64,64]{4,3,2,1,0:T(8,128)}) %all-gather.34.cloned.1.call-update) | async-done | bytes 3670032 | tf_op jit(solution)/shard_map/all_gather | solution.py:59
  1439.7 36.2 %fusion.133 = f32[1,64,64,64]{3,2,1,0:T(8,128)} fusion(f32[1,64,64,7]{3,2,1,0:T(8,128)} %get-tuple-element.14, f32[1,64,64,64]{3,2,1,0:T(8,128)S(1)} %fusion.166, f32[1,64,64,7]{3,2,1,0:T(8,128)} %get-tuple-element.13, f32[]{:T(128)} %bitcast.96, f32[]{:T(128)} %bitcast.95, f32[]{:T(128)} %bitcast.94, f32[]{:T(128)} %bitcast.93, f32[]{:T(128)} %bitcast.92, ...), kind=kLoop, calls=%fused_computation.210 | loop fusion | flops 11272192 | bytes 2326588 | tf_op jit(solution)/shard_map/add | solution.py:77
  1477.8 84.3 %all-gather.36.cloned.1.call-done = f32[16,2,3,64,64]{4,3,2,1,0:T(8,128)} async-done(((f32[1,2,3,64,64]{4,3,2,1,0:T(8,128)}), f32[16,2,3,64,64]{4,3,2,1,0:T(8,128)}) %all-gather.36.cloned.1.call-update) | async-done | bytes 1572880 | tf_op jit(solution)/shard_map/all_gather | solution.py:63
  1568.9 6.9 fusion.75
  1576.5 84.3 %all-gather.38.cloned.1.call-done = f32[16,2,3,64,64]{4,3,2,1,0:T(8,128)} async-done(((f32[1,2,3,64,64]{4,3,2,1,0:T(8,128)}), f32[16,2,3,64,64]{4,3,2,1,0:T(8,128)}) %all-gather.38.cloned.1.call-update) | async-done | bytes 1572880 | tf_op jit(solution)/shard_map/all_gather | solution.py:63
  1676.1 86.1 %reduce-scatter.2.cloned.1.call-done = f32[1,64,4,64]{3,1,0,2:T(8,128)} async-done(((f32[1,64,64,64]{3,1,0,2:T(8,128)}), f32[1,64,4,64]{3,1,0,2:T(8,128)}) %reduce-scatter.2.cloned.1.call-update) | async-done | bytes 65552 | tf_op jit(solution)/shard_map/reduce_scatter | solution.py:123
  (188 shorter events, 216.8 us)
Async XLA Ops:
  6.5 72.1 %copy-start.15 = (f32[1,7]{1,0:T(1,128)S(1)}, f32[1,7]{1,0:T(1,128)}, u32[]{:S(2)}) copy-start(f32[1,7]{1,0:T(1,128)} %param.9) | copy-start | bytes 88
  6.5 72.8 %copy-start.14 = (s32[1,6]{1,0:T(1,128)S(1)}, s32[1,6]{1,0:T(1,128)}, u32[]{:S(2)}) copy-start(s32[1,6]{1,0:T(1,128)} %param.12) | copy-start | bytes 76
  6.5 69.3 %all-gather.14.cloned.1.call-start = ((), (), s32[]{:S(2)}) async-start(), calls=%async_computation.1 | async-start | bytes 2228224 | tf_op jit(solution)/shard_map/all_gather | solution.py:102
  8.2 151.9 %all-gather.16.cloned.1.call-start = ((), (), s32[]{:S(2)}) async-start(), calls=%async_computation.2 | async-start | bytes 3342336 | tf_op jit(solution)/shard_map/all_gather | solution.py:47
  78.6 180.7 %all-gather.18.cloned.1.call-start = ((), (), s32[]{:S(2)}) async-start(), calls=%async_computation.3 | async-start | bytes 3342336 | tf_op jit(solution)/shard_map/all_gather | solution.py:51
  166.4 8.9 copy-start.16
  174.9 201.1 %all-gather.20.cloned.1.call-start = ((), (), s32[]{:S(2)}) async-start(), calls=%async_computation.4 | async-start | bytes 7798784 | tf_op jit(solution)/shard_map/all_gather | solution.py:55
  277.7 5.3 copy-start.17
  277.7 5.9 copy-start.13
  282.6 236.2 %all-gather.22.cloned.1.call-start = ((), (), s32[]{:S(2)}) async-start(), calls=%async_computation.5 | async-start | bytes 7798784 | tf_op jit(solution)/shard_map/all_gather | solution.py:59
  425.4 236.7 %all-gather.24.cloned.1.call-start = ((), (), s32[]{:S(2)}) async-start(), calls=%async_computation.6 | async-start | bytes 3342336 | tf_op jit(solution)/shard_map/all_gather | solution.py:63
  534.5 5.0 copy-start.3
  577.7 183.3 %all-gather.26.cloned.1.call-start = ((), (), s32[]{:S(2)}) async-start(), calls=%async_computation.7 | async-start | bytes 3342336 | tf_op jit(solution)/shard_map/all_gather | solution.py:63
  664.2 4.6 copy-start.8
  676.6 298.1 %all-reduce.2.cloned.1.call-start = ((), (), s32[]{:S(2)}) async-start(), calls=%async_computation.8 | async-start | bytes 4194304 | tf_op jit(solution)/shard_map/psum | solution.py:120
  774.9 287.1 %all-gather.28.cloned.1.call-start = ((), (), s32[]{:S(2)}) async-start(), calls=%async_computation.9 | async-start | bytes 3342336 | tf_op jit(solution)/shard_map/all_gather | solution.py:47
  978.3 90.0 %copy-start.6 = (f32[1,64,64,64]{3,2,1,0:T(8,128)}, f32[1,64,64,64]{3,2,1,0:T(8,128)S(1)}, u32[]{:S(2)}) copy-start(f32[1,64,64,64]{3,2,1,0:T(8,128)S(1)} %select_multiply_fusion) | copy-start | bytes 3145732
  979.1 182.1 %all-gather.30.cloned.1.call-start = ((), (), s32[]{:S(2)}) async-start(), calls=%async_computation.10 | async-start | bytes 3342336 | tf_op jit(solution)/shard_map/all_gather | solution.py:51
  1076.8 197.3 %all-gather.32.cloned.1.call-start = ((), (), s32[]{:S(2)}) async-start(), calls=%async_computation.11 | async-start | bytes 7798784 | tf_op jit(solution)/shard_map/all_gather | solution.py:55
  1163.3 4.6 copy-start.12
  1180.7 238.4 %all-gather.34.cloned.1.call-start = ((), (), s32[]{:S(2)}) async-start(), calls=%async_computation.12 | async-start | bytes 7798784 | tf_op jit(solution)/shard_map/all_gather | solution.py:59
  1325.8 236.4 %all-gather.36.cloned.1.call-start = ((), (), s32[]{:S(2)}) async-start(), calls=%async_computation.13 | async-start | bytes 3342336 | tf_op jit(solution)/shard_map/all_gather | solution.py:63
  1477.8 183.1 %all-gather.38.cloned.1.call-start = ((), (), s32[]{:S(2)}) async-start(), calls=%async_computation.14 | async-start | bytes 3342336 | tf_op jit(solution)/shard_map/all_gather | solution.py:63
  1576.5 185.7 %reduce-scatter.2.cloned.1.call-start = ((), (), s32[]{:S(2)}) async-start(), calls=%async_computation.15 | async-start | bytes 2228224 | tf_op jit(solution)/shard_map/reduce_scatter | solution.py:123
  (9 other events, 25.6 us)
Sparse Core Ops, SparseCore 0:
  10.0 65.7 all-gather.13
  78.7 81.3 all-gather.15
  175.0 84.2 all-gather.17
  282.7 93.2 all-gather.19
  425.5 93.2 all-gather.21
  577.9 84.2 all-gather.23
  676.8 84.2 all-gather.25
  775.0 199.6 all-reduce.1
  979.2 82.7 all-gather.27
  1076.9 84.2 all-gather.29
  1180.9 93.2 all-gather.31
  1325.9 93.2 all-gather.33
  1477.9 84.2 all-gather.35
  1576.6 84.2 all-gather.37
  1676.2 85.9 reduce-scatter.1
where the time goes:
time: 1780 us; the launch traced here: 1770 us
  waiting for transfers between devices  1380 us (78%)
  other arithmetic  190 us (11%)
  local copies, waits for them, and re-layouts  114 us (6%)
  matrix products  66 us (4%)
    all_gather x12, waiting for transfers between devices, with_halo(): lax.all_gather(edge_slabs, 'space', axis=0, tiled=True)  1030 us
    psum x1, waiting for transfers between devices, shards(): summed = lax.psum(spread, 'view')  199 us
    add x10, other arithmetic, convolve(): summed + weight * lax.slice_in_dim(extended, position, position + length,...  126 us
    reduce_scatter x1, waiting for transfers between devices, shards(): summed = lax.psum_scatter(spread, 'view', scatter_dimension=2, tiled=True)  86.1 us
    all_gather x1, waiting for transfers between devices, shards(): full_now = lax.all_gather(share_now, 'view', axis=2, tiled=True)  67.6 us
    div x2, other arithmetic, shards(): quotient = recorded_all[0] / blurred  48.4 us
  transfers between devices with their start and end apart: 15, of which 15 were waited for; matrix products, arithmetic and copies ran while one was open for 1% of the time, Pallas kernels for 0%

commit v1 on v0

--- a/solution.py
+++ b/solution.py
@@ -117,7 +117,7 @@
         spread = convolve(with_halo(spread, neighbors, 1, radius_x, "ratio"), along_x, 1, True)
         final_sweep = sweep_no == ITERS - 1
         if not final_sweep:
-            summed = lax.psum(spread, "view")
+            summed = jnp.sum(lax.all_gather(spread, "view"), axis=0)
             full_now = full_now * jnp.where(keep_mask, summed / view_count, 1.0)
         else:
             summed = lax.psum_scatter(spread, "view", scatter_dimension=2, tiled=True)

time: 1780 us -> 1900 us (1.067)
  waiting for transfers between devices: 1380 us -> 1490 us
    all_gather x0 -> x1, waiting for transfers between devices: none -> 307 us  [shards(): summed = jnp.sum(lax.all_gather(spread, 'view'), axis=0)]
    psum x1 -> x0, waiting for transfers between devices: 199 us -> none  [shards(): summed = lax.psum(spread, 'view')]
where the time goes in v1:
time: 1900 us; the launch traced here: 1890 us
  waiting for transfers between devices  1490 us (78%)
  other arithmetic  207 us (11%)
  local copies, waits for them, and re-layouts  114 us (6%)
  matrix products  67.1 us (4%)
    all_gather x12, waiting for transfers between devices, with_halo(): lax.all_gather(edge_slabs, 'space', axis=0, tiled=True)  1030 us
    all_gather x1, waiting for transfers between devices, shards(): summed = jnp.sum(lax.all_gather(spread, 'view'), axis=0)  307 us
    add x10, other arithmetic, convolve(): summed + weight * lax.slice_in_dim(extended, position, position + length,...  128 us
    reduce_scatter x1, waiting for transfers between devices, shards(): summed = lax.psum_scatter(spread, 'view', scatter_dimension=2, tiled=True)  86.1 us
    all_gather x1, waiting for transfers between devices, shards(): full_now = lax.all_gather(share_now, 'view', axis=2, tiled=True)  67.6 us
    div x2, other arithmetic, shards(): quotient = recorded_all[0] / blurred  48.8 us
  transfers between devices with their start and end apart: 15, of which 15 were waited for; matrix products, arithmetic and copies ran while one was open for 1% of the time, Pallas kernels for 0%

profile of v1, /device:TPU:8, one launch (start us, length us, event | category | flops | bytes accessed | tf_op | source)
XLA Modules:
  0.0 1893.3 jit_solution(8635521364183669051)
XLA Ops:
  8.3 67.6 %all-gather.16.cloned.1.call-done = f32[1,64,64,64]{3,1,0,2:T(8,128)} async-done(((f32[1,64,4,64]{3,1,0,2:T(8,128)}), f32[1,64,64,64]{3,1,0,2:T(8,128)}) %all-gather.16.cloned.1.call-update) | async-done | bytes 1048592 | tf_op jit(solution)/shard_map/all_gather | solution.py:102
  84.1 76.0 %all-gather.18.cloned.1.call-done = f32[16,2,3,64,64]{4,3,2,1,0:T(8,128)} async-done(((f32[1,2,3,64,64]{4,3,2,1,0:T(8,128)}), f32[16,2,3,64,64]{4,3,2,1,0:T(8,128)}) %all-gather.18.cloned.1.call-update) | async-done | bytes 1572880 | tf_op jit(solution)/shard_map/all_gather | solution.py:47
  177.3 82.0 %all-gather.20.cloned.1.call-done = f32[16,2,3,64,64]{4,3,2,1,0:T(8,128)} async-done(((f32[1,2,3,64,64]{4,3,2,1,0:T(8,128)}), f32[16,2,3,64,64]{4,3,2,1,0:T(8,128)}) %all-gather.20.cloned.1.call-update) | async-done | bytes 1572880 | tf_op jit(solution)/shard_map/all_gather | solution.py:51
  266.2 6.8 fusion.117
  287.7 88.8 %all-gather.22.cloned.1.call-done = f32[16,2,7,64,64]{4,3,2,1,0:T(8,128)} async-done(((f32[1,2,7,64,64]{4,3,2,1,0:T(8,128)}), f32[16,2,7,64,64]{4,3,2,1,0:T(8,128)}) %all-gather.22.cloned.1.call-update) | async-done | bytes 3670032 | tf_op jit(solution)/shard_map/all_gather | solution.py:55
  395.5 24.4 %fusion.239 = f32[1,64,64,64]{3,2,1,0:T(8,128)S(1)} fusion(f32[1,64,64,64]{3,2,1,0:T(8,128)S(1)} %copy-done.4, f32[1,64,64,7]{3,2,1,0:T(8,128)S(1)} %get-tuple-element.20, f32[1,64,64,64]{3,2,1,0:T(8,128)S(1)} %fusion.117, f32[1,64,64,7]{3,2,1,0:T(8,128)S(1)} %get-tuple-element.19, f32[]{:T(128)} %bitcast.96, f32[]{:T(128)} %bitcast.95, f32[]{:T(128)} %bitcast.94, ...), kind=kLoop, calls=%fused_computation.402 | loop fusion | flops 11534336 | bytes 3375164 | tf_op jit(solution)/shard_map/div | solution.py:114
  426.3 93.2 %all-gather.24.cloned.1.call-done = f32[16,2,7,64,64]{4,3,2,1,0:T(8,128)} async-done(((f32[1,2,7,64,64]{4,3,2,1,0:T(8,128)}), f32[16,2,7,64,64]{4,3,2,1,0:T(8,128)}) %all-gather.24.cloned.1.call-update) | async-done | bytes 3670032 | tf_op jit(solution)/shard_map/all_gather | solution.py:59
  540.2 36.7 %fusion.206 = f32[1,64,64,64]{3,2,1,0:T(8,128)} fusion(f32[1,64,64,7]{3,2,1,0:T(8,128)} %get-tuple-element.18, f32[1,64,64,64]{3,2,1,0:T(8,128)S(1)} %copy-done.3, f32[1,64,64,7]{3,2,1,0:T(8,128)} %get-tuple-element.17, f32[]{:T(128)} %bitcast.96, f32[]{:T(128)} %bitcast.95, f32[]{:T(128)} %bitcast.94, f32[]{:T(128)} %bitcast.93, f32[]{:T(128)} %bitcast.92, ...), kind=kLoop, calls=%fused_computation.343 | loop fusion | flops 11272192 | bytes 2326588 | tf_op jit(solution)/shard_map/add | solution.py:77
  578.8 84.3 %all-gather.26.cloned.1.call-done = f32[16,2,3,64,64]{4,3,2,1,0:T(8,128)} async-done(((f32[1,2,3,64,64]{4,3,2,1,0:T(8,128)}), f32[16,2,3,64,64]{4,3,2,1,0:T(8,128)}) %all-gather.26.cloned.1.call-update) | async-done | bytes 1572880 | tf_op jit(solution)/shard_map/all_gather | solution.py:63
  670.1 7.3 fusion.103
  678.1 84.3 %all-gather.28.cloned.1.call-done = f32[16,2,3,64,64]{4,3,2,1,0:T(8,128)} async-done(((f32[1,2,3,64,64]{4,3,2,1,0:T(8,128)}), f32[16,2,3,64,64]{4,3,2,1,0:T(8,128)}) %all-gather.28.cloned.1.call-update) | async-done | bytes 1572880 | tf_op jit(solution)/shard_map/all_gather | solution.py:63
  768.8 7.4 fusion.47
  776.9 307.0 %all-gather.42.cloned.1.call-done = f32[16,64,64,64]{3,2,1,0:T(8,128)} async-done(((f32[1,64,64,64]{3,2,1,0:T(8,128)}), f32[16,64,64,64]{3,2,1,0:T(8,128)}) %all-gather.42.cloned.1.call-update) | async-done | bytes 16777232 | tf_op jit(solution)/shard_map/all_gather | solution.py:120
  1083.9 14.2 reduce.4
  1102.5 80.1 %all-gather.30.cloned.1.call-done = f32[16,2,3,64,64]{4,3,2,1,0:T(8,128)} async-done(((f32[1,2,3,64,64]{4,3,2,1,0:T(8,128)}), f32[16,2,3,64,64]{4,3,2,1,0:T(8,128)}) %all-gather.30.cloned.1.call-update) | async-done | bytes 1572880 | tf_op jit(solution)/shard_map/all_gather | solution.py:47
  1197.8 84.3 %all-gather.32.cloned.1.call-done = f32[16,2,3,64,64]{4,3,2,1,0:T(8,128)} async-done(((f32[1,2,3,64,64]{4,3,2,1,0:T(8,128)}), f32[16,2,3,64,64]{4,3,2,1,0:T(8,128)}) %all-gather.32.cloned.1.call-update) | async-done | bytes 1572880 | tf_op jit(solution)/shard_map/all_gather | solution.py:51
  1302.2 93.1 %all-gather.34.cloned.1.call-done = f32[16,2,7,64,64]{4,3,2,1,0:T(8,128)} async-done(((f32[1,2,7,64,64]{4,3,2,1,0:T(8,128)}), f32[16,2,7,64,64]{4,3,2,1,0:T(8,128)}) %all-gather.34.cloned.1.call-update) | async-done | bytes 3670032 | tf_op jit(solution)/shard_map/all_gather | solution.py:55
  1414.7 24.4 %fusion.166 = f32[1,64,64,64]{3,2,1,0:T(8,128)S(1)} fusion(f32[1,64,64,64]{3,2,1,0:T(8,128)S(1)} %copy-done.5, f32[1,64,64,7]{3,2,1,0:T(8,128)S(1)} %get-tuple-element.16, f32[1,64,64,64]{3,2,1,0:T(8,128)S(1)} %copy-done.1, f32[1,64,64,7]{3,2,1,0:T(8,128)S(1)} %get-tuple-element.15, f32[]{:T(128)} %bitcast.96, f32[]{:T(128)} %bitcast.95, f32[]{:T(128)} %bitcast.94, ...), kind=kLoop, calls=%fused_computation.269 | loop fusion | flops 11534336 | bytes 3375164 | tf_op jit(solution)/shard_map/div | solution.py:114
  1447.9 92.9 %all-gather.36.cloned.1.call-done = f32[16,2,7,64,64]{4,3,2,1,0:T(8,128)} async-done(((f32[1,2,7,64,64]{4,3,2,1,0:T(8,128)}), f32[16,2,7,64,64]{4,3,2,1,0:T(8,128)}) %all-gather.36.cloned.1.call-update) | async-done | bytes 3670032 | tf_op jit(solution)/shard_map/all_gather | solution.py:59
  1561.3 36.7 %fusion.133 = f32[1,64,64,64]{3,2,1,0:T(8,128)} fusion(f32[1,64,64,7]{3,2,1,0:T(8,128)} %get-tuple-element.14, f32[1,64,64,64]{3,2,1,0:T(8,128)S(1)} %fusion.166, f32[1,64,64,7]{3,2,1,0:T(8,128)} %get-tuple-element.13, f32[]{:T(128)} %bitcast.96, f32[]{:T(128)} %bitcast.95, f32[]{:T(128)} %bitcast.94, f32[]{:T(128)} %bitcast.93, f32[]{:T(128)} %bitcast.92, ...), kind=kLoop, calls=%fused_computation.210 | loop fusion | flops 11272192 | bytes 2326588 | tf_op jit(solution)/shard_map/add | solution.py:77
  1599.9 84.3 %all-gather.38.cloned.1.call-done = f32[16,2,3,64,64]{4,3,2,1,0:T(8,128)} async-done(((f32[1,2,3,64,64]{4,3,2,1,0:T(8,128)}), f32[16,2,3,64,64]{4,3,2,1,0:T(8,128)}) %all-gather.38.cloned.1.call-update) | async-done | bytes 1572880 | tf_op jit(solution)/shard_map/all_gather | solution.py:63
  1691.2 7.1 fusion.75
  1699.0 84.3 %all-gather.40.cloned.1.call-done = f32[16,2,3,64,64]{4,3,2,1,0:T(8,128)} async-done(((f32[1,2,3,64,64]{4,3,2,1,0:T(8,128)}), f32[16,2,3,64,64]{4,3,2,1,0:T(8,128)}) %all-gather.40.cloned.1.call-update) | async-done | bytes 1572880 | tf_op jit(solution)/shard_map/all_gather | solution.py:63
  1798.6 86.1 %reduce-scatter.2.cloned.1.call-done = f32[1,64,4,64]{3,1,0,2:T(8,128)} async-done(((f32[1,64,64,64]{3,1,0,2:T(8,128)}), f32[1,64,4,64]{3,1,0,2:T(8,128)}) %reduce-scatter.2.cloned.1.call-update) | async-done | bytes 65552 | tf_op jit(solution)/shard_map/reduce_scatter | solution.py:123
  (189 shorter events, 224.8 us)
Async XLA Ops:
  6.5 72.1 %copy-start.15 = (f32[1,7]{1,0:T(1,128)S(1)}, f32[1,7]{1,0:T(1,128)}, u32[]{:S(2)}) copy-start(f32[1,7]{1,0:T(1,128)} %param.9) | copy-start | bytes 88
  6.5 72.8 %copy-start.14 = (s32[1,6]{1,0:T(1,128)S(1)}, s32[1,6]{1,0:T(1,128)}, u32[]{:S(2)}) copy-start(s32[1,6]{1,0:T(1,128)} %param.12) | copy-start | bytes 76
  6.5 69.3 %all-gather.16.cloned.1.call-start = ((), (), s32[]{:S(2)}) async-start(), calls=%async_computation.1 | async-start | bytes 2228224 | tf_op jit(solution)/shard_map/all_gather | solution.py:102
  8.2 151.9 %all-gather.18.cloned.1.call-start = ((), (), s32[]{:S(2)}) async-start(), calls=%async_computation.2 | async-start | bytes 3342336 | tf_op jit(solution)/shard_map/all_gather | solution.py:47
  78.6 180.7 %all-gather.20.cloned.1.call-start = ((), (), s32[]{:S(2)}) async-start(), calls=%async_computation.3 | async-start | bytes 3342336 | tf_op jit(solution)/shard_map/all_gather | solution.py:51
  166.4 8.9 copy-start.16
  175.0 201.5 %all-gather.22.cloned.1.call-start = ((), (), s32[]{:S(2)}) async-start(), calls=%async_computation.4 | async-start | bytes 7798784 | tf_op jit(solution)/shard_map/all_gather | solution.py:55
  278.2 5.3 copy-start.17
  278.2 6.0 copy-start.13
  283.1 236.3 %all-gather.24.cloned.1.call-start = ((), (), s32[]{:S(2)}) async-start(), calls=%async_computation.5 | async-start | bytes 7798784 | tf_op jit(solution)/shard_map/all_gather | solution.py:59
  426.1 237.1 %all-gather.26.cloned.1.call-start = ((), (), s32[]{:S(2)}) async-start(), calls=%async_computation.6 | async-start | bytes 3342336 | tf_op jit(solution)/shard_map/all_gather | solution.py:63
  535.2 4.9 copy-start.3
  578.8 183.7 %all-gather.28.cloned.1.call-start = ((), (), s32[]{:S(2)}) async-start(), calls=%async_computation.7 | async-start | bytes 3342336 | tf_op jit(solution)/shard_map/all_gather | solution.py:63
  665.3 4.8 copy-start.8
  678.1 405.8 %all-gather.42.cloned.1.call-start = ((), (), s32[]{:S(2)}) async-start(), calls=%async_computation.15 | async-start | bytes 35651584 | tf_op jit(solution)/shard_map/all_gather | solution.py:120
  776.2 406.4 %all-gather.30.cloned.1.call-start = ((), (), s32[]{:S(2)}) async-start(), calls=%async_computation.8 | async-start | bytes 3342336 | tf_op jit(solution)/shard_map/all_gather | solution.py:47
  1101.6 87.4 %copy-start.6 = (f32[1,64,64,64]{3,2,1,0:T(8,128)}, f32[1,64,64,64]{3,2,1,0:T(8,128)S(1)}, u32[]{:S(2)}) copy-start(f32[1,64,64,64]{3,2,1,0:T(8,128)S(1)} %bitcast_multiply_fusion) | copy-start | bytes 3145732
  1102.5 179.6 %all-gather.32.cloned.1.call-start = ((), (), s32[]{:S(2)}) async-start(), calls=%async_computation.9 | async-start | bytes 3342336 | tf_op jit(solution)/shard_map/all_gather | solution.py:51
  1197.7 197.7 %all-gather.34.cloned.1.call-start = ((), (), s32[]{:S(2)}) async-start(), calls=%async_computation.10 | async-start | bytes 7798784 | tf_op jit(solution)/shard_map/all_gather | solution.py:55
  1284.2 4.8 copy-start.12
  1302.0 238.8 %all-gather.36.cloned.1.call-start = ((), (), s32[]{:S(2)}) async-start(), calls=%async_computation.11 | async-start | bytes 7798784 | tf_op jit(solution)/shard_map/all_gather | solution.py:59
  1447.4 236.9 %all-gather.38.cloned.1.call-start = ((), (), s32[]{:S(2)}) async-start(), calls=%async_computation.12 | async-start | bytes 3342336 | tf_op jit(solution)/shard_map/all_gather | solution.py:63
  1599.9 183.5 %all-gather.40.cloned.1.call-start = ((), (), s32[]{:S(2)}) async-start(), calls=%async_computation.13 | async-start | bytes 3342336 | tf_op jit(solution)/shard_map/all_gather | solution.py:63
  1699.0 185.7 %reduce-scatter.2.cloned.1.call-start = ((), (), s32[]{:S(2)}) async-start(), calls=%async_computation.14 | async-start | bytes 2228224 | tf_op jit(solution)/shard_map/reduce_scatter | solution.py:123
  (9 other events, 25.9 us)
Sparse Core Ops, SparseCore 0:
  10.0 65.7 all-gather.15
  78.7 81.3 all-gather.17
  175.1 84.1 all-gather.19
  283.2 93.2 all-gather.21
  426.2 93.2 all-gather.23
  578.9 84.2 all-gather.25
  678.2 84.1 all-gather.27
  776.3 307.5 all-gather.41
  1102.6 80.0 all-gather.29
  1197.8 84.2 all-gather.31
  1302.1 93.2 all-gather.33
  1447.5 93.2 all-gather.35
  1600.0 84.2 all-gather.37
  1699.1 84.2 all-gather.39
  1798.7 85.9 reduce-scatter.1
